TPU v7x, 256 devices: a whole 4x4x8 slice. The times are simulated.
256 devices in a mesh: band: 16 (over z, x_hi), domain: 16 (over y, x_lo, core).
Axes of the slice: x: 4 (x_hi: 2, x_lo: 2; x = x_hi * 2 + x_lo), y: 4, z: 8, core: 2. Of those that a mesh axis runs over, the one named last changes fastest.
Arguments:
- orbitals: float32 [256, 16384], P('band', 'domain'), may hold values from -12 to 12
- potential: float32 [16384], P('domain'), may hold values from -9 to 4.5
- stencil: int32 [36, 16384], P(None, 'domain'), may hold values from 0 to 1536, as said below
- send_list: int32 [2, 4096], P(None, 'domain'), may hold values from 0 to 1023, as said below
- send_count: int32 [2, 16], P(None, 'domain'), may hold values from 0 to 256, as said below
Outputs:
- filtered: float32 [256, 16384], P('band', 'domain')
- correlation: float32 [256, 256], P('band', 'domain')
- subspace: float32 [256, 256], P('band', 'domain')
Inputs may be any that keep to these rules, and one draw needn't show every extreme that they name: `stencil`: entries below 1024 name a slot of the point's own subdomain; entries from 1024 on name only live boundary rows of an existing neighbouring subdomain; 1536 marks a neighbour outside the cluster. `send_list`: each list of 256 entries holds distinct slots of the sending subdomain. `send_count`: row 0 counts the rows subdomain d sends to d + 1, row 1 those it sends to d - 1; zero toward a missing neighbour; 256 is reached in every draw.
All inputs are finite; a program needn't handle non-finite values.
Results may differ from a plain program's by a relative error of at most 0.00015.
Values sent between devices are 32-bit elements; how exact they have to be, the bound alone decides.
No kernel may reach another device: no remote copies, remote signals or barrier semaphores. Data moves between devices by JAX's collectives and lax.ppermute only.
A program may use at most 128 MiB of HBM per device.

v0:
```python
import jax
import jax.numpy as jnp
from jax import lax
from jax.sharding import PartitionSpec as P

DEGREE = 4
WEIGHTS = (
    -5369.0 / 1800.0,
    12.0 / 7.0,
    -15.0 / 56.0,
    10.0 / 189.0,
    -1.0 / 112.0,
    2.0 / 1925.0,
    -1.0 / 16632.0,
)
KINETIC = 50.0 / 9.0
CUT_SHARE = 0.1
SPECTRAL_REACH = (
    KINETIC
    * 3.0
    * (
        abs(WEIGHTS[0])
        + 2.0
        * (
            abs(WEIGHTS[1])
            + abs(WEIGHTS[2])
            + abs(WEIGHTS[3])
            + abs(WEIGHTS[4])
            + abs(WEIGHTS[5])
            + abs(WEIGHTS[6])
        )
    )
)


def with_halo(block, sides, width):
    for axis, dim in sides:
        count = lax.axis_size(axis)
        forward = [(i, i + 1) for i in range(count - 1)]
        backward = [(target, source) for source, target in forward]
        low = lax.ppermute(
            lax.slice_in_dim(block, block.shape[dim] - width, None, axis=dim), axis, forward
        )
        high = lax.ppermute(lax.slice_in_dim(block, 0, width, axis=dim), axis, backward)
        block = jnp.concatenate([low, block, high], axis=dim)
    return block


def apply_operator(values, potential, stencil, send_list, live_slots):
    capacity = send_list.shape[1]
    sent_rows = values[:, send_list]
    sent_rows = jnp.where(live_slots[None], sent_rows, jnp.zeros_like(sent_rows))
    outgoing = jnp.concatenate([sent_rows[:, 1], sent_rows[:, 0]], axis=1)
    padded = with_halo(outgoing, (("domain", 1),), capacity)
    from_below = padded[:, :capacity]
    from_above = padded[:, 3 * capacity :]
    zero_column = jnp.zeros((values.shape[0], 1), values.dtype)
    buffer = jnp.concatenate([values, from_below, from_above, zero_column], axis=1)
    near_sum = jnp.zeros_like(values)
    for distance in range(6):
        cycle_sum = jnp.zeros_like(values)
        for member in range(6):
            cycle_sum = cycle_sum + buffer[:, stencil[6 * distance + member]]
        near_sum = near_sum + WEIGHTS[distance + 1] * cycle_sum
    return potential * values - KINETIC * (3.0 * WEIGHTS[0] * values + near_sum)


def filter_block(orbitals, operator_fn, lowest, highest):
    top_bound = highest + SPECTRAL_REACH
    cut_point = lowest + CUT_SHARE * (top_bound - lowest)
    half_width = (top_bound - cut_point) / 2.0
    centre = (top_bound + cut_point) / 2.0
    sigma_now = half_width / (lowest - centre)
    sigma_scale = 2.0 / sigma_now
    previous = orbitals
    current = sigma_now / half_width * (operator_fn(orbitals) - centre * orbitals)
    for order_index in range(2, DEGREE + 1):
        sigma_next = 1.0 / (sigma_scale - sigma_now)
        following = (
            2.0 * sigma_next / half_width * (operator_fn(current) - centre * current)
            - sigma_now * sigma_next * previous
        )
        previous = current
        current = following
        sigma_now = sigma_next
    return current


def inner_products(left_block, right_block):
    return lax.dot_general(
        left_block,
        right_block,
        (((1,), (1,)), ((), ())),
        precision=lax.Precision.HIGHEST,
        preferred_element_type=jnp.float32,
    )


def shards(orbitals, potential, stencil, send_list, send_count):
    points = orbitals.shape[1]
    capacity = send_list.shape[1]
    domain_count = lax.axis_size("domain")
    total_points = points * domain_count
    lowest = lax.pmin(jnp.min(potential), "domain")
    highest = lax.pmax(jnp.max(potential), "domain")
    live_slots = lax.broadcasted_iota(jnp.int32, (2, capacity), 1) < send_count

    def operator_fn(values):
        return apply_operator(values, potential, stencil, send_list, live_slots)

    filtered = filter_block(orbitals, operator_fn, lowest, highest)
    applied = operator_fn(filtered)
    piece_values = lax.all_gather(filtered, "band", axis=0, tiled=True)
    piece_applied = lax.all_gather(applied, "band", axis=0, tiled=True)
    correlation_part = inner_products(filtered, piece_values)
    subspace_part = inner_products(filtered, piece_applied)
    correlation_part, subspace_part = (correlation_part, subspace_part)
    correlation_sum, subspace_sum = (
        lax.psum_scatter(correlation_part, "domain", scatter_dimension=1, tiled=True),
        lax.psum_scatter(subspace_part, "domain", scatter_dimension=1, tiled=True),
    )
    return (filtered, correlation_sum / total_points, subspace_sum / total_points)


def solution(mesh):
    placed = (
        P("band", "domain"),
        P("domain"),
        P(None, "domain"),
        P(None, "domain"),
        P(None, "domain"),
    )
    return jax.shard_map(
        shards,
        mesh=mesh,
        in_specs=placed,
        out_specs=(P("band", "domain"), P("band", "domain"), P("band", "domain")),
        check_vma=False,
    )
```

profile of v0, /device:TPU:4, one launch (start us, length us, event | category | flops | bytes accessed | tf_op | source)
XLA Modules:
  0.0 1158.1 jit_solution(5905052475874954502)
XLA Ops:
  16.9 32.3 %pmax.7 = f32[]{:T(128)} all-reduce(f32[]{:T(128)} %get-tuple-element.19), channel_id=1, replica_groups=mesh['band'=16,'domain'=16] {'domain'}, use_global_device_ids=true, to_apply=%region_3.0 | all-reduce | flops 1 | bytes 8 | tf_op jit(solution)/shard_map/pmax | solution.py:105
  49.2 27.8 %pmin.7 = f32[]{:T(128)} all-reduce(f32[]{:T(128)} %get-tuple-element.18), channel_id=1, replica_groups=mesh['band'=16,'domain'=16] {'domain'}, use_global_device_ids=true, to_apply=%region_1.0 | all-reduce | flops 1 | bytes 8 | tf_op jit(solution)/shard_map/pmin | solution.py:104
  201.8 4.0 gather_fusion.54
  209.8 4.0 gather_fusion.56
  229.7 4.0 gather_fusion.61
  233.7 4.0 gather_fusion.62
  237.7 4.0 gather_fusion.63
  257.7 4.0 gather_fusion.68
  261.7 4.0 gather_fusion.69
  269.7 4.0 gather_fusion.71
  297.6 4.0 gather_fusion.45
  301.6 4.0 gather_fusion.46
  397.6 4.0 gather_fusion.91
  405.6 4.0 gather_fusion.93
  425.6 4.0 gather_fusion.98
  429.6 4.0 gather_fusion.99
  433.6 4.0 gather_fusion.100
  453.5 4.0 gather_fusion.105
  457.5 4.0 gather_fusion.106
  465.5 4.0 gather_fusion.108
  493.5 4.0 gather_fusion.82
  497.5 4.0 gather_fusion.83
  589.5 4.0 gather_fusion.113
  597.5 4.0 gather_fusion.129
  601.5 4.0 gather_fusion.130
  617.4 4.0 gather_fusion.134
  621.4 4.0 gather_fusion.135
  629.4 4.0 gather_fusion.137
  645.4 4.0 gather_fusion.141
  657.4 4.0 gather_fusion.144
  661.4 4.0 gather_fusion.145
  693.3 4.0 gather_fusion.120
  697.3 4.0 gather_fusion.121
  796.9 4.0 gather_fusion.169
  804.8 4.0 gather_fusion.171
  808.8 4.0 gather_fusion.172
  836.8 4.0 gather_fusion.179
  844.8 4.0 gather_fusion.181
  856.7 4.0 gather_fusion.151
  868.7 4.0 gather_fusion.154
  872.7 4.0 gather_fusion.155
  876.7 4.0 gather_fusion.156
  896.7 4.0 gather_fusion.161
  908.7 4.0 gather_fusion.164
  912.7 4.0 gather_fusion.183
  944.3 76.7 %all-gather.5.cloned.1.call-done = f32[256,1024]{1,0:T(8,128)} async-done(((f32[16,1024]{1,0:T(8,128)}), f32[256,1024]{1,0:T(8,128)}) %all-gather.5.cloned.1.call-update) | async-done | bytes 1048592 | tf_op jit(solution)/shard_map/all_gather | solution.py:114
  1023.9 61.8 %reduce-scatter.7.cloned.1.call-done = f32[16,16]{1,0:T(8,128)} async-done(((f32[256,16]{1,0:T(8,128)}), f32[16,16]{1,0:T(8,128)}) %reduce-scatter.7.cloned.1.call-update) | async-done | bytes 1040
  1087.1 62.9 %reduce-scatter.9.cloned.1.call-done = f32[16,16]{1,0:T(8,128)} async-done(((f32[256,16]{1,0:T(8,128)}), f32[16,16]{1,0:T(8,128)}) %reduce-scatter.9.cloned.1.call-update) | async-done | bytes 1040
  (1115 shorter events, 705.3 us)
Async XLA Ops:
  7.2 934.3 %all-gather.3.cloned.1.call-start = ((), (), s32[]{:S(2)}) async-start(), calls=%async_computation.2 | async-start | bytes 1114112 | tf_op jit(solution)/shard_map/all_gather | solution.py:113
  11.4 68.0 %collective-permute-start = (f32[16,256]{1,0:T(8,128)S(1)}, f32[16,256]{1,0:T(8,128)S(1)}, u32[]{:S(2)}, u32[]{:S(2)}) collective-permute-start(f32[16,256]{1,0:T(8,128)S(1)} %get-tuple-element.64), channel_id=1, source_target_pairs={{0,1},{1,2},{2,3},{3,4},{4,5},{5,6},{6,7},{7,8},{8,9},{9,10},{10,1... | collective-permute-start | bytes 49160 | tf_op jit(solution)/shard_map/ppermute | solution.py:41
  13.2 66.4 %collective-permute-start.1 = (f32[16,256]{1,0:T(8,128)S(1)}, f32[16,256]{1,0:T(8,128)S(1)}, u32[]{:S(2)}, u32[]{:S(2)}) collective-permute-start(f32[16,256]{1,0:T(8,128)S(1)} %get-tuple-element.65), channel_id=1, source_target_pairs={{1,0},{2,1},{3,2},{4,3},{5,4},{6,5},{7,6},{8,7},{9,8},{10,9},{11,1... | collective-permute-start | bytes 49160 | tf_op jit(solution)/shard_map/ppermute | solution.py:44
  14.8 71.2 %copy-start.159 = (s32[1024]{0:T(1024)}, s32[1024]{0:T(1024)S(1)}, u32[]{:S(2)}) copy-start(s32[1024]{0:T(1024)S(1)} %broadcast_clamp_fusion.18) | copy-start | bytes 12292
  14.8 74.2 %copy-start.164 = (s32[1024]{0:T(1024)}, s32[1024]{0:T(1024)S(1)}, u32[]{:S(2)}) copy-start(s32[1024]{0:T(1024)S(1)} %broadcast_clamp_fusion.17) | copy-start | bytes 12292
  14.8 77.1 %copy-start.169 = (s32[1024]{0:T(1024)}, s32[1024]{0:T(1024)S(1)}, u32[]{:S(2)}) copy-start(s32[1024]{0:T(1024)S(1)} %broadcast_clamp_fusion.16) | copy-start | bytes 12292
  14.8 80.1 %copy-start.174 = (s32[1024]{0:T(1024)}, s32[1024]{0:T(1024)S(1)}, u32[]{:S(2)}) copy-start(s32[1024]{0:T(1024)S(1)} %broadcast_clamp_fusion.15) | copy-start | bytes 12292
  14.9 83.1 %copy-start.179 = (s32[1024]{0:T(1024)}, s32[1024]{0:T(1024)S(1)}, u32[]{:S(2)}) copy-start(s32[1024]{0:T(1024)S(1)} %broadcast_clamp_fusion.14) | copy-start | bytes 12292
  14.9 86.0 %copy-start.184 = (s32[1024]{0:T(1024)}, s32[1024]{0:T(1024)S(1)}, u32[]{:S(2)}) copy-start(s32[1024]{0:T(1024)S(1)} %broadcast_clamp_fusion.13) | copy-start | bytes 12292
  14.9 89.0 %copy-start.189 = (s32[1024]{0:T(1024)}, s32[1024]{0:T(1024)S(1)}, u32[]{:S(2)}) copy-start(s32[1024]{0:T(1024)S(1)} %broadcast_clamp_fusion.12) | copy-start | bytes 12292
  14.9 92.0 %copy-start.194 = (s32[1024]{0:T(1024)}, s32[1024]{0:T(1024)S(1)}, u32[]{:S(2)}) copy-start(s32[1024]{0:T(1024)S(1)} %broadcast_clamp_fusion.11) | copy-start | bytes 12292
  14.9 94.9 %copy-start.199 = (s32[1024]{0:T(1024)}, s32[1024]{0:T(1024)S(1)}, u32[]{:S(2)}) copy-start(s32[1024]{0:T(1024)S(1)} %broadcast_clamp_fusion.10) | copy-start | bytes 12292
  15.0 97.9 %copy-start.204 = (s32[1024]{0:T(1024)}, s32[1024]{0:T(1024)S(1)}, u32[]{:S(2)}) copy-start(s32[1024]{0:T(1024)S(1)} %broadcast_clamp_fusion.9) | copy-start | bytes 12292
  15.0 100.9 %copy-start.209 = (s32[1024]{0:T(1024)}, s32[1024]{0:T(1024)S(1)}, u32[]{:S(2)}) copy-start(s32[1024]{0:T(1024)S(1)} %broadcast_clamp_fusion.8) | copy-start | bytes 12292
  15.0 103.8 %copy-start.214 = (s32[1024]{0:T(1024)}, s32[1024]{0:T(1024)S(1)}, u32[]{:S(2)}) copy-start(s32[1024]{0:T(1024)S(1)} %broadcast_clamp_fusion.7) | copy-start | bytes 12292
  15.0 106.8 %copy-start.219 = (s32[1024]{0:T(1024)}, s32[1024]{0:T(1024)S(1)}, u32[]{:S(2)}) copy-start(s32[1024]{0:T(1024)S(1)} %broadcast_clamp_fusion.6) | copy-start | bytes 12292
  15.1 109.8 %copy-start.224 = (s32[1024]{0:T(1024)}, s32[1024]{0:T(1024)S(1)}, u32[]{:S(2)}) copy-start(s32[1024]{0:T(1024)S(1)} %broadcast_clamp_fusion.5) | copy-start | bytes 12292
  15.1 112.7 %copy-start.229 = (s32[1024]{0:T(1024)}, s32[1024]{0:T(1024)S(1)}, u32[]{:S(2)}) copy-start(s32[1024]{0:T(1024)S(1)} %broadcast_clamp_fusion.4) | copy-start | bytes 12292
  15.1 115.7 %copy-start.234 = (s32[1024]{0:T(1024)}, s32[1024]{0:T(1024)S(1)}, u32[]{:S(2)}) copy-start(s32[1024]{0:T(1024)S(1)} %broadcast_clamp_fusion.3) | copy-start | bytes 12292
  15.1 118.7 %copy-start.239 = (s32[1024]{0:T(1024)}, s32[1024]{0:T(1024)S(1)}, u32[]{:S(2)}) copy-start(s32[1024]{0:T(1024)S(1)} %broadcast_clamp_fusion.2) | copy-start | bytes 12292
  15.1 121.6 %copy-start.244 = (s32[1024]{0:T(1024)}, s32[1024]{0:T(1024)S(1)}, u32[]{:S(2)}) copy-start(s32[1024]{0:T(1024)S(1)} %broadcast_clamp_fusion.35) | copy-start | bytes 12292
  15.2 124.6 %copy-start.249 = (s32[1024]{0:T(1024)}, s32[1024]{0:T(1024)S(1)}, u32[]{:S(2)}) copy-start(s32[1024]{0:T(1024)S(1)} %broadcast_clamp_fusion.33) | copy-start | bytes 12292
  15.2 127.6 %copy-start.254 = (s32[1024]{0:T(1024)}, s32[1024]{0:T(1024)S(1)}, u32[]{:S(2)}) copy-start(s32[1024]{0:T(1024)S(1)} %broadcast_clamp_fusion.32) | copy-start | bytes 12292
  15.2 130.5 %copy-start.259 = (s32[1024]{0:T(1024)}, s32[1024]{0:T(1024)S(1)}, u32[]{:S(2)}) copy-start(s32[1024]{0:T(1024)S(1)} %broadcast_clamp_fusion.31) | copy-start | bytes 12292
  15.2 133.5 %copy-start.264 = (s32[1024]{0:T(1024)}, s32[1024]{0:T(1024)S(1)}, u32[]{:S(2)}) copy-start(s32[1024]{0:T(1024)S(1)} %broadcast_clamp_fusion.30) | copy-start | bytes 12292
  15.3 136.5 %copy-start.269 = (s32[1024]{0:T(1024)}, s32[1024]{0:T(1024)S(1)}, u32[]{:S(2)}) copy-start(s32[1024]{0:T(1024)S(1)} %broadcast_clamp_fusion.29) | copy-start | bytes 12292
  15.3 139.4 %copy-start.274 = (s32[1024]{0:T(1024)}, s32[1024]{0:T(1024)S(1)}, u32[]{:S(2)}) copy-start(s32[1024]{0:T(1024)S(1)} %broadcast_clamp_fusion.28) | copy-start | bytes 12292
  15.3 142.4 %copy-start.279 = (s32[1024]{0:T(1024)}, s32[1024]{0:T(1024)S(1)}, u32[]{:S(2)}) copy-start(s32[1024]{0:T(1024)S(1)} %broadcast_clamp_fusion.27) | copy-start | bytes 12292
  15.3 145.4 %copy-start.284 = (s32[1024]{0:T(1024)}, s32[1024]{0:T(1024)S(1)}, u32[]{:S(2)}) copy-start(s32[1024]{0:T(1024)S(1)} %broadcast_clamp_fusion.26) | copy-start | bytes 12292
  15.4 148.3 %copy-start.289 = (s32[1024]{0:T(1024)}, s32[1024]{0:T(1024)S(1)}, u32[]{:S(2)}) copy-start(s32[1024]{0:T(1024)S(1)} %broadcast_clamp_fusion.25) | copy-start | bytes 12292
  15.4 151.3 %copy-start.294 = (s32[1024]{0:T(1024)}, s32[1024]{0:T(1024)S(1)}, u32[]{:S(2)}) copy-start(s32[1024]{0:T(1024)S(1)} %broadcast_clamp_fusion.24) | copy-start | bytes 12292
  15.4 154.3 %copy-start.299 = (s32[1024]{0:T(1024)}, s32[1024]{0:T(1024)S(1)}, u32[]{:S(2)}) copy-start(s32[1024]{0:T(1024)S(1)} %broadcast_clamp_fusion.23) | copy-start | bytes 12292
  15.4 157.2 %copy-start.304 = (s32[1024]{0:T(1024)}, s32[1024]{0:T(1024)S(1)}, u32[]{:S(2)}) copy-start(s32[1024]{0:T(1024)S(1)} %broadcast_clamp_fusion.22) | copy-start | bytes 12292
  15.4 160.2 %copy-start.309 = (s32[1024]{0:T(1024)}, s32[1024]{0:T(1024)S(1)}, u32[]{:S(2)}) copy-start(s32[1024]{0:T(1024)S(1)} %broadcast_clamp_fusion.21) | copy-start | bytes 12292
  15.5 163.2 %copy-start.314 = (s32[1024]{0:T(1024)}, s32[1024]{0:T(1024)S(1)}, u32[]{:S(2)}) copy-start(s32[1024]{0:T(1024)S(1)} %broadcast_clamp_fusion.20) | copy-start | bytes 12292
  15.5 166.8 %copy-start.319 = (s32[1024]{0:T(1024)}, s32[1024]{0:T(1024)S(1)}, u32[]{:S(2)}) copy-start(s32[1024]{0:T(1024)S(1)} %broadcast_clamp_fusion.1) | copy-start | bytes 12292
  16.2 169.7 %copy-start.324 = (s32[1024]{0:T(1024)}, s32[1024]{0:T(1024)S(1)}, u32[]{:S(2)}) copy-start(s32[1024]{0:T(1024)S(1)} %broadcast_clamp_fusion) | copy-start | bytes 12292
  192.2 3.4 collective-permute-start.2
  194.0 3.1 collective-permute-start.3
  385.9 5.5 collective-permute-start.4
  389.9 3.1 collective-permute-start.5
  581.8 5.7 collective-permute-start.6
  585.7 3.1 collective-permute-start.7
  772.2 248.8 %all-gather.5.cloned.1.call-start = ((), (), s32[]{:S(2)}) async-start(), calls=%async_computation.3 | async-start | bytes 1114112 | tf_op jit(solution)/shard_map/all_gather | solution.py:114
  775.0 5.4 collective-permute-start.8
  778.9 3.1 collective-permute-start.9
  941.4 144.4 %reduce-scatter.7.cloned.1.call-start = ((), (), s32[]{:S(2)}) async-start(), calls=%async_computation.4 | async-start | bytes 139264
  944.3 205.8 %reduce-scatter.9.cloned.1.call-start = ((), (), s32[]{:S(2)}) async-start(), calls=%async_computation.5 | async-start | bytes 139264
  (305 other events, 908.6 us)
Sparse Core Ops, SparseCore 0:
  772.3 78.6 all-gather.2
  941.5 79.5 all-gather.4
  1023.6 62.1 reduce-scatter.6
  1088.1 61.9 reduce-scatter.8
where the time goes:
time: 1170 us; the launch traced here: 1160 us
  local copies, waits for them, and re-layouts  837 us (72%)
  waiting for transfers between devices  207 us (18%)
  blocking collectives  60.1 us (5%)
  starting transfers between devices  22.8 us (2%)
  between operations  19.4 us (2%)
    gather x360, local copies, waits for them, and re-layouts, apply_operator(): cycle_sum = cycle_sum + buffer[:, stencil[6 * distance + member]]  804 us
    unnamed x6, waiting for transfers between devices  125 us
    all_gather x1, waiting for transfers between devices, shards(): piece_applied = lax.all_gather(applied, 'band', axis=0, tiled=True)  76.7 us
    pmax x1, blocking collectives, shards(): highest = lax.pmax(jnp.max(potential), 'domain')  32.3 us
    pmin x1, blocking collectives, shards(): lowest = lax.pmin(jnp.min(potential), 'domain')  27.8 us
    unnamed x682, local copies, waits for them, and re-layouts  25.6 us
  transfers between devices with their start and end apart: 14, of which 7 were waited for; matrix products, arithmetic and copies ran while one was open for 14% of the time, Pallas kernels for 0%

commit v1 on v0

--- a/solution.py
+++ b/solution.py
@@ -1,3 +1,4 @@
+import functools
 import jax
 import jax.numpy as jnp
 from jax import lax
@@ -31,6 +32,21 @@
         )
     )
 )
+
+
+def perform_the_surface(arr_in, which_axis):
+    return jnp.concatenate(
+        lax.all_to_all(
+            jnp.stack(lax.axis_size(which_axis) * [arr_in], 0),
+            axis_name=which_axis,
+            split_axis=0,
+            concat_axis=0,
+        ),
+        0,
+    )
+
+
+pair_notes = functools.partial(perform_the_surface, which_axis="band")
 
 
 def with_halo(block, sides, width):
@@ -111,7 +127,7 @@
     filtered = filter_block(orbitals, operator_fn, lowest, highest)
     applied = operator_fn(filtered)
     piece_values = lax.all_gather(filtered, "band", axis=0, tiled=True)
-    piece_applied = lax.all_gather(applied, "band", axis=0, tiled=True)
+    piece_applied = pair_notes(applied)
     correlation_part = inner_products(filtered, piece_values)
     subspace_part = inner_products(filtered, piece_applied)
     correlation_part, subspace_part = (correlation_part, subspace_part)

time: 1170 us -> 1110 us (0.949)
  waiting for transfers between devices: 207 us -> 134 us
    all_gather x1 -> x0, waiting for transfers between devices: 76.7 us -> none  [shards(): piece_applied = lax.all_gather(applied, 'band', axis=0, tiled=True)]
    all_to_all x0 -> x1, waiting for transfers between devices: none -> 22.9 us  [perform_the_surface(): lax.all_to_all(jnp.stack(lax.axis_size(which_axis) * [arr_in], 0), axis_n...]
    unnamed x6 -> x5, waiting for transfers between devices: 125 us -> 105 us
    unnamed x682 -> x686, local copies, waits for them, and re-layouts: 25.6 us -> 25.4 us
where the time goes in v1:
time: 1110 us; the launch traced here: 1100 us
  local copies, waits for them, and re-layouts  844 us (76%)
  waiting for transfers between devices  134 us (12%)
  blocking collectives  60.1 us (5%)
  starting transfers between devices  34.3 us (3%)
  between operations  19.5 us (2%)
    gather x360, local copies, waits for them, and re-layouts, apply_operator(): cycle_sum = cycle_sum + buffer[:, stencil[6 * distance + member]]  810 us
    unnamed x5, waiting for transfers between devices  105 us
    pmax x1, blocking collectives, shards(): highest = lax.pmax(jnp.max(potential), 'domain')  32.4 us
    pmin x1, blocking collectives, shards(): lowest = lax.pmin(jnp.min(potential), 'domain')  27.8 us
    unnamed x686, local copies, waits for them, and re-layouts  25.4 us
    all_to_all x1, waiting for transfers between devices, perform_the_surface(): lax.all_to_all(jnp.stack(lax.axis_size(which_axis) * [arr_in], 0), axis_n...  22.9 us
  transfers between devices with their start and end apart: 14, of which 7 were waited for; matrix products, arithmetic and copies ran while one was open for 14% of the time, Pallas kernels for 0%

profile of v1, /device:TPU:4, one launch (start us, length us, event | category | flops | bytes accessed | tf_op | source)
XLA Modules:
  0.0 1100.3 jit_solution(12916155106275560654)
XLA Ops:
  16.8 32.4 %pmax.7 = f32[]{:T(128)} all-reduce(f32[]{:T(128)} %get-tuple-element.19), channel_id=1, replica_groups=mesh['band'=16,'domain'=16] {'domain'}, use_global_device_ids=true, to_apply=%region_3.0 | all-reduce | flops 1 | bytes 8 | tf_op jit(solution)/shard_map/pmax | solution.py:121
  49.2 27.8 %pmin.7 = f32[]{:T(128)} all-reduce(f32[]{:T(128)} %get-tuple-element.18), channel_id=1, replica_groups=mesh['band'=16,'domain'=16] {'domain'}, use_global_device_ids=true, to_apply=%region_1.0 | all-reduce | flops 1 | bytes 8 | tf_op jit(solution)/shard_map/pmin | solution.py:120
  197.9 4.0 gather_fusion.39
  209.9 4.0 gather_fusion.56
  238.1 4.0 gather_fusion.63
  262.3 4.0 gather_fusion.69
  266.3 4.1 gather_fusion.70
  270.4 4.0 gather_fusion.71
  274.4 4.0 gather_fusion.38
  298.6 4.0 gather_fusion.45
  310.6 4.0 gather_fusion.48
  314.7 4.0 gather_fusion.49
  395.0 4.0 gather_fusion.76
  407.1 4.0 gather_fusion.93
  435.3 4.0 gather_fusion.100
  459.5 4.0 gather_fusion.106
  463.5 4.1 gather_fusion.107
  467.6 4.0 gather_fusion.108
  471.6 4.0 gather_fusion.75
  495.8 4.0 gather_fusion.82
  507.8 4.0 gather_fusion.85
  511.9 4.0 gather_fusion.86
  592.2 4.0 gather_fusion.113
  604.3 4.0 gather_fusion.130
  608.4 4.0 gather_fusion.131
  636.5 4.0 gather_fusion.138
  660.7 4.0 gather_fusion.144
  664.8 4.0 gather_fusion.145
  668.8 4.1 gather_fusion.112
  672.9 4.0 gather_fusion.114
  697.0 4.0 gather_fusion.120
  709.1 4.0 gather_fusion.123
  713.1 4.0 gather_fusion.124
  778.7 4.0 collective-permute-start.8
  800.7 4.0 gather_fusion.169
  812.8 4.0 gather_fusion.172
  837.0 4.0 gather_fusion.178
  841.0 4.0 gather_fusion.179
  845.0 4.1 gather_fusion.180
  849.1 4.0 gather_fusion.181
  873.3 4.0 gather_fusion.154
  901.5 4.0 gather_fusion.161
  909.5 4.0 gather_fusion.163
  913.6 4.0 gather_fusion.164
  946.8 11.4 %all-to-all-start = ((f32[16,16,1024]{2,1,0:T(8,128)}), f32[16,16,1024]{2,1,0:T(8,128)S(1)}, u32[]{:S(2)}, u32[]{:S(2)}) async-start(f32[16,16,1024]{2,1,0:T(8,128)} %stack.2), calls=%async_computation | async-start | bytes 2097152 | tf_op jit(solution)/shard_map/all_to_all | solution.py:39
  961.3 22.9 %all-to-all-done = f32[16,16,1024]{2,1,0:T(8,128)S(1)} async-done(((f32[16,16,1024]{2,1,0:T(8,128)}), f32[16,16,1024]{2,1,0:T(8,128)S(1)}, u32[]{:S(2)}, u32[]{:S(2)}) %all-to-all-start) | async-done | bytes 1048608 | tf_op jit(solution)/shard_map/all_to_all | solution.py:39
  985.8 40.2 %reduce-scatter.7.cloned.1.call-done = f32[16,16]{1,0:T(8,128)} async-done(((f32[256,16]{1,0:T(8,128)}), f32[16,16]{1,0:T(8,128)}) %reduce-scatter.7.cloned.1.call-update) | async-done | bytes 1040
  1027.3 64.9 %reduce-scatter.9.cloned.1.call-done = f32[16,16]{1,0:T(8,128)} async-done(((f32[256,16]{1,0:T(8,128)}), f32[16,16]{1,0:T(8,128)}) %reduce-scatter.9.cloned.1.call-update) | async-done | bytes 1040
  (1119 shorter events, 711.7 us)
Async XLA Ops:
  7.2 951.2 %all-gather.2.cloned.1.call-start = ((), (), s32[]{:S(2)}) async-start(), calls=%async_computation.3 | async-start | bytes 1114112 | tf_op jit(solution)/shard_map/all_gather | solution.py:129
  11.4 68.1 %collective-permute-start = (f32[16,256]{1,0:T(8,128)S(1)}, f32[16,256]{1,0:T(8,128)S(1)}, u32[]{:S(2)}, u32[]{:S(2)}) collective-permute-start(f32[16,256]{1,0:T(8,128)S(1)} %get-tuple-element.64), channel_id=1, source_target_pairs={{0,1},{1,2},{2,3},{3,4},{4,5},{5,6},{6,7},{7,8},{8,9},{9,10},{10,1... | collective-permute-start | bytes 49160 | tf_op jit(solution)/shard_map/ppermute | solution.py:57
  13.2 66.5 %collective-permute-start.1 = (f32[16,256]{1,0:T(8,128)S(1)}, f32[16,256]{1,0:T(8,128)S(1)}, u32[]{:S(2)}, u32[]{:S(2)}) collective-permute-start(f32[16,256]{1,0:T(8,128)S(1)} %get-tuple-element.65), channel_id=1, source_target_pairs={{1,0},{2,1},{3,2},{4,3},{5,4},{6,5},{7,6},{8,7},{9,8},{10,9},{11,1... | collective-permute-start | bytes 49160 | tf_op jit(solution)/shard_map/ppermute | solution.py:60
  14.8 71.2 %copy-start.161 = (s32[1024]{0:T(1024)}, s32[1024]{0:T(1024)S(1)}, u32[]{:S(2)}) copy-start(s32[1024]{0:T(1024)S(1)} %broadcast_clamp_fusion.18) | copy-start | bytes 12292
  14.8 74.2 %copy-start.166 = (s32[1024]{0:T(1024)}, s32[1024]{0:T(1024)S(1)}, u32[]{:S(2)}) copy-start(s32[1024]{0:T(1024)S(1)} %broadcast_clamp_fusion.17) | copy-start | bytes 12292
  14.8 77.2 %copy-start.171 = (s32[1024]{0:T(1024)}, s32[1024]{0:T(1024)S(1)}, u32[]{:S(2)}) copy-start(s32[1024]{0:T(1024)S(1)} %broadcast_clamp_fusion.16) | copy-start | bytes 12292
  14.8 80.1 %copy-start.176 = (s32[1024]{0:T(1024)}, s32[1024]{0:T(1024)S(1)}, u32[]{:S(2)}) copy-start(s32[1024]{0:T(1024)S(1)} %broadcast_clamp_fusion.15) | copy-start | bytes 12292
  14.9 83.1 %copy-start.181 = (s32[1024]{0:T(1024)}, s32[1024]{0:T(1024)S(1)}, u32[]{:S(2)}) copy-start(s32[1024]{0:T(1024)S(1)} %broadcast_clamp_fusion.14) | copy-start | bytes 12292
  14.9 86.1 %copy-start.186 = (s32[1024]{0:T(1024)}, s32[1024]{0:T(1024)S(1)}, u32[]{:S(2)}) copy-start(s32[1024]{0:T(1024)S(1)} %broadcast_clamp_fusion.13) | copy-start | bytes 12292
  14.9 89.0 %copy-start.191 = (s32[1024]{0:T(1024)}, s32[1024]{0:T(1024)S(1)}, u32[]{:S(2)}) copy-start(s32[1024]{0:T(1024)S(1)} %broadcast_clamp_fusion.12) | copy-start | bytes 12292
  14.9 92.0 %copy-start.196 = (s32[1024]{0:T(1024)}, s32[1024]{0:T(1024)S(1)}, u32[]{:S(2)}) copy-start(s32[1024]{0:T(1024)S(1)} %broadcast_clamp_fusion.11) | copy-start | bytes 12292
  14.9 95.0 %copy-start.201 = (s32[1024]{0:T(1024)}, s32[1024]{0:T(1024)S(1)}, u32[]{:S(2)}) copy-start(s32[1024]{0:T(1024)S(1)} %broadcast_clamp_fusion.10) | copy-start | bytes 12292
  15.0 97.9 %copy-start.206 = (s32[1024]{0:T(1024)}, s32[1024]{0:T(1024)S(1)}, u32[]{:S(2)}) copy-start(s32[1024]{0:T(1024)S(1)} %broadcast_clamp_fusion.9) | copy-start | bytes 12292
  15.0 100.9 %copy-start.211 = (s32[1024]{0:T(1024)}, s32[1024]{0:T(1024)S(1)}, u32[]{:S(2)}) copy-start(s32[1024]{0:T(1024)S(1)} %broadcast_clamp_fusion.8) | copy-start | bytes 12292
  15.0 103.9 %copy-start.216 = (s32[1024]{0:T(1024)}, s32[1024]{0:T(1024)S(1)}, u32[]{:S(2)}) copy-start(s32[1024]{0:T(1024)S(1)} %broadcast_clamp_fusion.7) | copy-start | bytes 12292
  15.0 106.8 %copy-start.221 = (s32[1024]{0:T(1024)}, s32[1024]{0:T(1024)S(1)}, u32[]{:S(2)}) copy-start(s32[1024]{0:T(1024)S(1)} %broadcast_clamp_fusion.6) | copy-start | bytes 12292
  15.1 109.8 %copy-start.226 = (s32[1024]{0:T(1024)}, s32[1024]{0:T(1024)S(1)}, u32[]{:S(2)}) copy-start(s32[1024]{0:T(1024)S(1)} %broadcast_clamp_fusion.5) | copy-start | bytes 12292
  15.1 112.8 %copy-start.231 = (s32[1024]{0:T(1024)}, s32[1024]{0:T(1024)S(1)}, u32[]{:S(2)}) copy-start(s32[1024]{0:T(1024)S(1)} %broadcast_clamp_fusion.4) | copy-start | bytes 12292
  15.1 115.7 %copy-start.236 = (s32[1024]{0:T(1024)}, s32[1024]{0:T(1024)S(1)}, u32[]{:S(2)}) copy-start(s32[1024]{0:T(1024)S(1)} %broadcast_clamp_fusion.3) | copy-start | bytes 12292
  15.1 118.7 %copy-start.241 = (s32[1024]{0:T(1024)}, s32[1024]{0:T(1024)S(1)}, u32[]{:S(2)}) copy-start(s32[1024]{0:T(1024)S(1)} %broadcast_clamp_fusion.2) | copy-start | bytes 12292
  15.2 121.7 %copy-start.246 = (s32[1024]{0:T(1024)}, s32[1024]{0:T(1024)S(1)}, u32[]{:S(2)}) copy-start(s32[1024]{0:T(1024)S(1)} %broadcast_clamp_fusion.35) | copy-start | bytes 12292
  15.2 124.6 %copy-start.251 = (s32[1024]{0:T(1024)}, s32[1024]{0:T(1024)S(1)}, u32[]{:S(2)}) copy-start(s32[1024]{0:T(1024)S(1)} %broadcast_clamp_fusion.33) | copy-start | bytes 12292
  15.2 127.6 %copy-start.256 = (s32[1024]{0:T(1024)}, s32[1024]{0:T(1024)S(1)}, u32[]{:S(2)}) copy-start(s32[1024]{0:T(1024)S(1)} %broadcast_clamp_fusion.32) | copy-start | bytes 12292
  15.2 130.6 %copy-start.261 = (s32[1024]{0:T(1024)}, s32[1024]{0:T(1024)S(1)}, u32[]{:S(2)}) copy-start(s32[1024]{0:T(1024)S(1)} %broadcast_clamp_fusion.31) | copy-start | bytes 12292
  15.2 133.5 %copy-start.266 = (s32[1024]{0:T(1024)}, s32[1024]{0:T(1024)S(1)}, u32[]{:S(2)}) copy-start(s32[1024]{0:T(1024)S(1)} %broadcast_clamp_fusion.30) | copy-start | bytes 12292
  15.3 136.5 %copy-start.271 = (s32[1024]{0:T(1024)}, s32[1024]{0:T(1024)S(1)}, u32[]{:S(2)}) copy-start(s32[1024]{0:T(1024)S(1)} %broadcast_clamp_fusion.29) | copy-start | bytes 12292
  15.3 139.5 %copy-start.276 = (s32[1024]{0:T(1024)}, s32[1024]{0:T(1024)S(1)}, u32[]{:S(2)}) copy-start(s32[1024]{0:T(1024)S(1)} %broadcast_clamp_fusion.28) | copy-start | bytes 12292
  15.3 142.4 %copy-start.281 = (s32[1024]{0:T(1024)}, s32[1024]{0:T(1024)S(1)}, u32[]{:S(2)}) copy-start(s32[1024]{0:T(1024)S(1)} %broadcast_clamp_fusion.27) | copy-start | bytes 12292
  15.3 145.4 %copy-start.286 = (s32[1024]{0:T(1024)}, s32[1024]{0:T(1024)S(1)}, u32[]{:S(2)}) copy-start(s32[1024]{0:T(1024)S(1)} %broadcast_clamp_fusion.26) | copy-start | bytes 12292
  15.4 148.4 %copy-start.291 = (s32[1024]{0:T(1024)}, s32[1024]{0:T(1024)S(1)}, u32[]{:S(2)}) copy-start(s32[1024]{0:T(1024)S(1)} %broadcast_clamp_fusion.25) | copy-start | bytes 12292
  15.4 151.3 %copy-start.296 = (s32[1024]{0:T(1024)}, s32[1024]{0:T(1024)S(1)}, u32[]{:S(2)}) copy-start(s32[1024]{0:T(1024)S(1)} %broadcast_clamp_fusion.24) | copy-start | bytes 12292
  15.4 154.3 %copy-start.301 = (s32[1024]{0:T(1024)}, s32[1024]{0:T(1024)S(1)}, u32[]{:S(2)}) copy-start(s32[1024]{0:T(1024)S(1)} %broadcast_clamp_fusion.23) | copy-start | bytes 12292
  15.4 157.3 %copy-start.306 = (s32[1024]{0:T(1024)}, s32[1024]{0:T(1024)S(1)}, u32[]{:S(2)}) copy-start(s32[1024]{0:T(1024)S(1)} %broadcast_clamp_fusion.22) | copy-start | bytes 12292
  15.4 160.2 %copy-start.311 = (s32[1024]{0:T(1024)}, s32[1024]{0:T(1024)S(1)}, u32[]{:S(2)}) copy-start(s32[1024]{0:T(1024)S(1)} %broadcast_clamp_fusion.21) | copy-start | bytes 12292
  15.5 163.2 %copy-start.316 = (s32[1024]{0:T(1024)}, s32[1024]{0:T(1024)S(1)}, u32[]{:S(2)}) copy-start(s32[1024]{0:T(1024)S(1)} %broadcast_clamp_fusion.20) | copy-start | bytes 12292
  15.5 166.8 %copy-start.321 = (s32[1024]{0:T(1024)}, s32[1024]{0:T(1024)S(1)}, u32[]{:S(2)}) copy-start(s32[1024]{0:T(1024)S(1)} %broadcast_clamp_fusion.1) | copy-start | bytes 12292
  16.2 169.7 %copy-start.326 = (s32[1024]{0:T(1024)}, s32[1024]{0:T(1024)S(1)}, u32[]{:S(2)}) copy-start(s32[1024]{0:T(1024)S(1)} %broadcast_clamp_fusion) | copy-start | bytes 12292
  192.3 3.4 collective-permute-start.2
  194.1 3.1 collective-permute-start.3
  387.4 5.5 collective-permute-start.4
  391.3 3.1 collective-permute-start.5
  584.6 5.7 collective-permute-start.6
  588.5 3.1 collective-permute-start.7
  778.7 5.5 collective-permute-start.8
  782.8 3.1 collective-permute-start.9
  946.8 37.3 %all-to-all-start = ((f32[16,16,1024]{2,1,0:T(8,128)}), f32[16,16,1024]{2,1,0:T(8,128)S(1)}, u32[]{:S(2)}, u32[]{:S(2)}) async-start(f32[16,16,1024]{2,1,0:T(8,128)} %stack.2), calls=%async_computation | async-start | bytes 2097152 | tf_op jit(solution)/shard_map/all_to_all | solution.py:39
  958.3 67.7 %reduce-scatter.7.cloned.1.call-start = ((), (), s32[]{:S(2)}) async-start(), calls=%async_computation.4 | async-start | bytes 139264
  961.2 131.0 %reduce-scatter.9.cloned.1.call-start = ((), (), s32[]{:S(2)}) async-start(), calls=%async_computation.5 | async-start | bytes 139264
  (307 other events, 921.9 us)
Sparse Core Ops, SparseCore 0:
  784.4 78.6 all-gather.1
  961.6 64.3 reduce-scatter.6
  1028.4 63.7 reduce-scatter.8
